TPU v7x, 256 devices: a whole 4x4x8 slice. The times are simulated.
256 devices in a mesh: row: 16 (over z_hi, x, core), col: 16 (over y, z_lo).
Axes of the slice: x: 4, y: 4, z: 8 (z_hi: 2, z_lo: 4; z = z_hi * 4 + z_lo), core: 2. Of those that a mesh axis runs over, the one named last changes fastest.
Arguments:
- points: float32 [64, 32768], P(None, ('row', 'col')), may hold values from -24 to 24, as said below
- embedding: float32 [2, 32768], P(None, ('row', 'col')), may hold values from -8 to 8
- precision: float32 [32768], P(('row', 'col')), may hold values from 0.05 to 2
Outputs:
- force: float32 [2, 32768], P(None, ('row', 'col'))
- calibrated: float32 [32768], P(('row', 'col'))
Inputs may be any that keep to these rules, and one draw needn't show every extreme that they name: `points`: each point's coordinates are normal values times a positive scale of that point.
All inputs are finite; a program needn't handle non-finite values.
Results may differ from a plain program's by a relative error of at most 0.0003.
Values sent between devices are 32-bit elements; how exact they have to be, the bound alone decides.
No kernel may reach another device: no remote copies, remote signals or barrier semaphores. Data moves between devices by JAX's collectives and lax.ppermute only.
A program may use at most 64 MiB of HBM per device.

v0:
```python
import math
import jax
import jax.numpy as jnp
from jax import lax
from jax.sharding import PartitionSpec as P

PERP = 30


def newton_update(zsum, first, second, start_prec):
    entropy = jnp.log(zsum) + start_prec * first / zsum
    spread = second / zsum - (first / zsum) ** 2
    factor = jnp.clip(
        (entropy - math.log(PERP)) / jnp.maximum(start_prec * start_prec * spread, 1.0), -2.0, 2.0
    )
    return start_prec * jnp.exp(factor)


def body(points, embedding, precision):
    per_dev = points.shape[1]
    width = points.shape[0]
    col_count = lax.axis_size("col")
    row_count = lax.axis_size("row")
    packed = jnp.concatenate([points, embedding, precision[None, :]], axis=0)
    row_pack = lax.all_gather(packed, "col", axis=1, tiled=True)
    col_pack = lax.all_gather(packed, "row", axis=1, tiled=True)
    rows_total = per_dev * col_count
    cols_total = per_dev * row_count
    total = rows_total * row_count
    row_coords = row_pack[:width]
    col_coords = col_pack[:width]
    row_map = row_pack[width : width + 2]
    col_map = col_pack[width : width + 2]
    row_prec = row_pack[width + 2]
    row_sq = jnp.sum(row_coords * row_coords, axis=0)
    col_sq = jnp.sum(col_coords * col_coords, axis=0)
    row_ids = lax.axis_index("row") * rows_total + jnp.arange(rows_total, dtype=jnp.int32)
    col_pos = jnp.arange(cols_total, dtype=jnp.int32)
    col_ids = col_pos // per_dev * rows_total + lax.axis_index("col") * per_dev + col_pos % per_dev
    block_rows = min(rows_total, 256)
    blocks = rows_total // block_rows
    own_start = lax.axis_index("col") * per_dev

    def slice_rows(values, start):
        return lax.dynamic_slice_in_dim(values, start, block_rows, values.ndim - 1)

    def distances(start):
        part = slice_rows(row_coords, start)
        inner = lax.dot_general(
            part,
            col_coords,
            (((0,), (0,)), ((), ())),
            precision=lax.Precision.HIGHEST,
            preferred_element_type=jnp.float32,
        )
        distance = jnp.maximum(
            slice_rows(row_sq, start)[:, None] + col_sq[None, :] - 2.0 * inner, 0.0
        )
        itself = slice_rows(row_ids, start)[:, None] == col_ids[None, :]
        return (distance, itself)

    def kernel_of(start, itself):
        part_y = slice_rows(row_map, start)
        delta_a = part_y[0][:, None] - col_map[0][None, :]
        delta_b = part_y[1][:, None] - col_map[1][None, :]
        return (jnp.where(itself, 0.0, 1.0 / (1.0 + delta_a * delta_a + delta_b * delta_b)), part_y)

    def sweep(step_fn, init):

        def wrapped(carry, index):
            return step_fn(carry, index * block_rows)

        carry, result = lax.scan(wrapped, init, jnp.arange(blocks, dtype=jnp.int32))
        return (carry, result.transpose(1, 0, 2).reshape(result.shape[1], rows_total))

    def nearest_step(carry, start):
        distance, itself = distances(start)
        masked = jnp.where(itself, jnp.inf, distance)
        return (carry, jnp.min(masked, axis=1)[None])

    col_min_part, row_min_part = sweep(nearest_step, jnp.full((cols_total,), jnp.inf, jnp.float32))
    nearest_rows = lax.pmin(row_min_part[0], "col")

    def moment_step(carry, start):
        distance, itself = distances(start)
        shifted = distance - slice_rows(nearest_rows, start)[:, None]
        expo = jnp.where(itself, 0.0, jnp.exp(-slice_rows(row_prec, start)[:, None] * shifted))
        row_part = jnp.stack(
            [
                jnp.sum(expo, axis=1),
                jnp.sum(expo * shifted, axis=1),
                jnp.sum(expo * shifted * shifted, axis=1),
            ]
        )
        return (carry, row_part)

    col_moment, row_moment = sweep(moment_step, jnp.zeros((3, cols_total), jnp.float32))
    row_z, row_first, row_second = lax.psum((row_moment[0], row_moment[1], row_moment[2]), "col")
    calib_rows = newton_update(row_z, row_first, row_second, row_prec)

    def norm_step(carry, start):
        distance, itself = distances(start)
        shifted = distance - slice_rows(nearest_rows, start)[:, None]
        row_part = jnp.sum(
            jnp.where(itself, 0.0, jnp.exp(-slice_rows(calib_rows, start)[:, None] * shifted)),
            axis=1,
        )
        return (carry, row_part[None])

    col_norm_part, row_norm_part = sweep(norm_step, jnp.zeros((cols_total,), jnp.float32))
    norm_rows = lax.psum(row_norm_part[0], "col")
    own_stats = jnp.stack(
        [
            lax.dynamic_slice_in_dim(calib_rows, own_start, per_dev, 0),
            lax.dynamic_slice_in_dim(nearest_rows, own_start, per_dev, 0),
            lax.dynamic_slice_in_dim(norm_rows, own_start, per_dev, 0),
        ]
    )
    col_stats = lax.all_gather(own_stats, "row", axis=1, tiled=True)
    calib_cols = col_stats[0]
    nearest_cols = col_stats[1]
    norm_cols = col_stats[2]

    def kernel_step(carry, index):
        start = index * block_rows
        itself = slice_rows(row_ids, start)[:, None] == col_ids[None, :]
        kernel, part_y = kernel_of(start, itself)
        return (carry + jnp.sum(kernel), None)

    kernel_part, unused = lax.scan(
        kernel_step, jnp.zeros((), jnp.float32), jnp.arange(blocks, dtype=jnp.int32)
    )
    qsum = lax.psum(kernel_part, ("row", "col"))

    def pulled(coef, part_y):
        moved = lax.dot_general(
            col_map,
            coef,
            (((1,), (1,)), ((), ())),
            precision=lax.Precision.HIGHEST,
            preferred_element_type=jnp.float32,
        )
        return part_y * jnp.sum(coef, axis=1)[None, :] - moved

    def force_step(carry, start):
        distance, itself = distances(start)
        kernel, part_y = kernel_of(start, itself)
        cond_rows = (
            jnp.exp(
                -slice_rows(calib_rows, start)[:, None]
                * (distance - slice_rows(nearest_rows, start)[:, None])
            )
            / slice_rows(norm_rows, start)[:, None]
        )
        cond_cols = (
            jnp.exp(-calib_cols[None, :] * (distance - nearest_cols[None, :])) / norm_cols[None, :]
        )
        affinity = jnp.where(itself, 0.0, 0.5 * (cond_rows + cond_cols))
        coef = (affinity - total * kernel / qsum) * kernel
        return (carry, pulled(coef, part_y))

    kernel_late, force_rows = sweep(force_step, jnp.zeros((), jnp.float32))
    force = lax.psum_scatter(force_rows, "col", scatter_dimension=1, tiled=True)
    calibrated = lax.dynamic_slice_in_dim(calib_rows, own_start, per_dev, 0)
    return (force, calibrated)


def solution(mesh):
    in_specs = (P(None, ("row", "col")), P(None, ("row", "col")), P(("row", "col")))
    out_specs = (P(None, ("row", "col")), P(("row", "col")))
    return jax.shard_map(body, mesh=mesh, in_specs=in_specs, out_specs=out_specs, check_vma=False)
```

profile of v0, /device:TPU:4, one launch (start us, length us, event | category | flops | bytes accessed | tf_op | source)
XLA Modules:
  0.0 634.6 jit_solution(9365061002655801085)
XLA Ops:
  8.0 49.5 %all_gather.9 = f32[67,2048]{1,0:T(8,128)S(1)} all-gather(f32[67,128]{1,0:T(8,128)S(1)} %pad_maximum_fusion), channel_id=1, replica_groups=mesh['row'=16,'col'=16] {'col'}, dimensions={1}, use_global_device_ids=true | all-gather | bytes 583168 | tf_op jit(solution)/shard_map/all_gather | solution.py:25
  57.5 25.0 %all_gather.10 = f32[67,2048]{1,0:T(8,128)S(1)} all-gather(f32[67,128]{1,0:T(8,128)S(1)} %pad_maximum_fusion), channel_id=1, replica_groups=mesh['row'=16,'col'=16] {'row'}, dimensions={1}, use_global_device_ids=true | all-gather | bytes 583168 | tf_op jit(solution)/shard_map/all_gather | solution.py:26
  83.3 31.0 %while.57 = (s32[]{:T(128)}, f32[8,1,256]{2,1,0:T(1,128)S(1)}, s32[8]{0:T(128)S(1)}, s32[2048]{0:T(1024)S(1)}, f32[2048]{0:T(1024)S(1)}, /*index=5*/f32[2048]{0:...) while((s32[]{:T(128)}, f32[8,1,256]{2,1,0:T(1,128)S(1)}, ...), condition=%wide.region_4.5_spmd.clone, body=%wide.region_2.4_spmd.clone.sunk | while | flops 406353664 | bytes 623819 | solution.py:73
  114.3 38.7 %pmin.7 = f32[2048]{0:T(1024)S(1)} all-reduce(f32[2048]{0:T(1024)S(1)} %bitcast.134), channel_id=1, replica_groups=mesh['row'=16,'col'=16] {'col'}, use_global_device_ids=true, to_apply=%region_5.6 | all-reduce | flops 2048 | bytes 16384 | tf_op jit(solution)/shard_map/pmin | solution.py:82
  153.0 34.9 %while.58 = (s32[]{:T(128)}, f32[8,3,256]{2,1,0:T(4,128)S(1)}, s32[8]{0:T(128)S(1)}, s32[2048]{0:T(1024)S(1)}, f32[2048]{0:T(1024)S(1)}, /*index=5*/f32[2048]{0:...) while((s32[]{:T(128)}, f32[8,3,256]{2,1,0:T(4,128)S(1)}, ...), condition=%wide.region_10.11_spmd.clone, body=%wide.region_6.10_spmd.clone.sunk | while | flops 409500672 | bytes 637155 | solution.py:73
  163.2 2.9 fusion.133
  176.2 2.9 fusion.133
  185.0 2.9 fusion.133
  188.0 76.5 %all-reduce = (f32[2048]{0:T(1024)S(1)}, f32[2048]{0:T(1024)S(1)}, f32[2048]{0:T(1024)S(1)}) all-reduce(f32[2048]{0:T(1024)S(1)} %bitcast.132, f32[2048]{0:T(1024)S(1)} %bitcast.133, f32[2048]{0:T(1024)S(1)} %bitcast.131), channel_id=1, replica_groups=mesh['row'=16,'col'=16] {'col'}, use_global_device_ids=true, to_apply=%region_12.13 | all-reduce | flops 6144 | bytes 49152 | tf_op jit(solution)/shard_map/psum | solution.py:98
  264.6 33.4 %while.59 = (s32[]{:T(128)}, f32[8,1,256]{2,1,0:T(1,128)S(1)}, s32[8]{0:T(128)S(1)}, s32[2048]{0:T(1024)S(1)}, f32[2048]{0:T(1024)S(1)}, /*index=5*/f32[2048]{0:...) while((s32[]{:T(128)}, f32[8,1,256]{2,1,0:T(1,128)S(1)}, ...), condition=%wide.region_16.17_spmd.clone, body=%wide.region_14.16_spmd.clone.sunk | while | flops 407402496 | bytes 629987 | solution.py:73
  298.0 38.7 %psum.38 = f32[2048]{0:T(1024)S(1)} all-reduce(f32[2048]{0:T(1024)S(1)} %bitcast.135), channel_id=1, replica_groups=mesh['row'=16,'col'=16] {'col'}, use_global_device_ids=true, to_apply=%region_17.18 | all-reduce | flops 2048 | bytes 16384 | tf_op jit(solution)/shard_map/psum | solution.py:111
  336.9 24.7 %all_gather.11 = f32[3,2048]{1,0:T(4,128)S(1)} all-gather(f32[3,128]{1,0:T(4,128)S(1)} %pad_maximum_fusion.1), channel_id=1, replica_groups=mesh['row'=16,'col'=16] {'row'}, dimensions={1}, use_global_device_ids=true | all-gather | bytes 26112 | tf_op jit(solution)/shard_map/all_gather | solution.py:119
  361.7 34.7 %while.60 = (s32[]{:T(128)}, f32[]{:T(128)}, s32[8]{0:T(128)S(1)}, s32[2048]{0:T(1024)S(1)}, f32[2,2048]{1,0:T(2,128)S(1)}, /*index=5*/f32[2,2048]{1,0:T(2,128)S...) while((s32[]{:T(128)}, f32[]{:T(128)}, s32[8]{0:T(128)S(1)}, ...), condition=%wide.region_20.21_spmd.clone, body=%wide.region_18.20_spmd.clone.sunk | while | flops 5273607 | bytes 74971 | solution.py:130
  396.4 79.2 %psum.39 = f32[]{:T(128)} all-reduce(f32[]{:T(128)} %get-tuple-element.407), channel_id=1, replica_groups=mesh['row'=16,'col'=16] {'row','col'}, use_global_device_ids=true, to_apply=%region_21.22 | all-reduce | flops 1 | bytes 8 | tf_op jit(solution)/shard_map/psum | solution.py:133
  475.6 65.4 %while.61 = (s32[]{:T(128)}, f32[8,2,256]{2,1,0:T(2,128)S(1)}, s32[8]{0:T(128)S(1)}, f32[2,2048]{1,0:T(2,128)S(1)}, s32[2048]{0:T(1024)S(1)}, /*index=5*/f32[204...) while((s32[]{:T(128)}, f32[8,2,256]{2,1,0:T(2,128)S(1)}, ...), condition=%wide.region_24.25_spmd.clone, body=%wide.region_22.24_spmd.clone.sunk | while | flops 429423616 | bytes 4926787 | solution.py:73
  477.4 4.6 fusion.146
  485.6 4.6 fusion.146
  493.8 4.6 fusion.146
  502.0 4.6 fusion.146
  510.2 4.6 fusion.146
  518.4 4.6 fusion.146
  526.5 4.6 fusion.146
  534.7 4.6 fusion.146
  543.0 83.2 %reduce-scatter.4.cloned.1.call-done = f32[128,2]{1,0:T(8,128)} async-done(((f32[2048,2]{1,0:T(8,128)}), f32[128,2]{1,0:T(8,128)}) %reduce-scatter.4.cloned.1.call-update) | async-done | bytes 1040
  (335 shorter events, 126.7 us)
Async XLA Ops:
  7.2 619.1 %reduce-scatter.4.cloned.1.call-start = ((), (), s32[]{:S(2)}) async-start(), calls=%async_computation.1 | async-start | bytes 1114112
  57.5 25.2 %copy-start.1 = (f32[67,2048]{1,0:T(8,128)}, f32[67,2048]{1,0:T(8,128)S(1)}, u32[]{:S(2)}) copy-start(f32[67,2048]{1,0:T(8,128)S(1)} %all_gather.9) | copy-start | bytes 1646596
  82.5 0.8 copy-start
  264.6 97.1 %slice-start = ((f32[67,2048]{1,0:T(8,128)}), f32[2,2048]{1,0:T(2,128)S(1)}, s32[]{:S(2)}) async-start(f32[67,2048]{1,0:T(8,128)} %copy-done), calls=%async_computation.2 | async-start | bytes 32768 | tf_op jit(solution)/shard_map/slice | solution.py:33
  264.6 97.1 %slice-start.1 = ((f32[67,2048]{1,0:T(8,128)}), f32[2,2048]{1,0:T(2,128)S(1)}, s32[]{:S(2)}) async-start(f32[67,2048]{1,0:T(8,128)} %copy-done.1), calls=%async_computation.3 | async-start | bytes 32768 | tf_op jit(solution)/shard_map/slice | solution.py:32
Sparse Core Ops, SparseCore 0:
  542.6 83.6 reduce-scatter.3
where the time goes:
time: 635 us
  blocking collectives  332 us (52%)
  matrix products  113 us (18%)
  waiting for transfers between devices  83.3 us (13%)
  local copies, waits for them, and re-layouts  39.3 us (6%)
  loops' own time  32.9 us (5%)
  other arithmetic  19.9 us (3%)
  between operations  14.2 us (2%)
    dot_general x32, matrix products, distances(): lax.dot_general(part, col_coords, (((0,), (0,)), ((), ())), precision=lax...  98.7 us
    unnamed x2, waiting for transfers between devices  83.3 us
    psum x1, blocking collectives, body(): qsum = lax.psum(kernel_part, ('row', 'col'))  79.2 us
    psum x1, blocking collectives, body(): lax.psum((row_moment[0], row_moment[1], row_moment[2]), 'col')  76.5 us
    all_gather x1, blocking collectives, body(): row_pack = lax.all_gather(packed, 'col', axis=1, tiled=True)  49.5 us
    psum x1, blocking collectives, body(): norm_rows = lax.psum(row_norm_part[0], 'col')  38.7 us
    pmin x1, blocking collectives, body(): nearest_rows = lax.pmin(row_min_part[0], 'col')  38.7 us
    dynamic_slice x40, local copies, waits for them, and re-layouts, sweep(): carry, result = lax.scan(wrapped, init, jnp.arange(blocks, dtype=jnp.int32))  25.5 us
  transfers between devices with their start and end apart: 1, of which 1 were waited for; matrix products, arithmetic and copies ran while one was open for 0% of the time, Pallas kernels for 0%

commit v1 on v0

--- a/solution.py
+++ b/solution.py
@@ -22,7 +22,9 @@
     col_count = lax.axis_size("col")
     row_count = lax.axis_size("row")
     packed = jnp.concatenate([points, embedding, precision[None, :]], axis=0)
-    row_pack = lax.all_gather(packed, "col", axis=1, tiled=True)
+    row_pack = jnp.concatenate(
+        lax.all_to_all(jnp.stack([packed] * lax.axis_size("col")), "col", 0, 0), axis=1
+    )
     col_pack = lax.all_gather(packed, "row", axis=1, tiled=True)
     rows_total = per_dev * col_count
     cols_total = per_dev * row_count

time: 635 us -> 602 us (0.948)
  blocking collectives: 332 us -> 291 us
  starting transfers between devices: 0.04 us -> 8.68 us
    all_gather x1 -> x0, blocking collectives: 49.5 us -> none  [body(): row_pack = lax.all_gather(packed, 'col', axis=1, tiled=True)]
    all_to_all x0 -> x1, starting transfers between devices: none -> 8.64 us  [body(): lax.all_to_all(jnp.stack([packed] * lax.axis_size('col')), 'col', 0, 0)]
    pmin x1, blocking collectives: 38.7 us -> 45.2 us  [body(): nearest_rows = lax.pmin(row_min_part[0], 'col')]
  transfers between devices with their start and end apart: 1 -> 2, of which waited for: 1 -> 1; matrix products, arithmetic and copies ran while one was open for 0% -> 0% of each run, Pallas kernels for 0% -> 0%
where the time goes in v1:
time: 602 us; the launch traced here: 601 us
  blocking collectives  291 us (48%)
  matrix products  113 us (19%)
  waiting for transfers between devices  84.3 us (14%)
  local copies, waits for them, and re-layouts  39.2 us (7%)
  loops' own time  31.2 us (5%)
  other arithmetic  19.9 us (3%)
  between operations  14.2 us (2%)
  starting transfers between devices  8.68 us (1%)
    dot_general x32, matrix products, distances(): lax.dot_general(part, col_coords, (((0,), (0,)), ((), ())), precision=lax...  99 us
    unnamed x2, waiting for transfers between devices  84.3 us
    psum x1, blocking collectives, body(): qsum = lax.psum(kernel_part, ('row', 'col'))  77.2 us
    psum x1, blocking collectives, body(): lax.psum((row_moment[0], row_moment[1], row_moment[2]), 'col')  74.6 us
    pmin x1, blocking collectives, body(): nearest_rows = lax.pmin(row_min_part[0], 'col')  45.2 us
    psum x1, blocking collectives, body(): norm_rows = lax.psum(row_norm_part[0], 'col')  38.8 us
    all_gather x1, blocking collectives, body(): col_stats = lax.all_gather(own_stats, 'row', axis=1, tiled=True)  28 us
    all_gather x1, blocking collectives, body(): col_pack = lax.all_gather(packed, 'row', axis=1, tiled=True)  26.6 us
  transfers between devices with their start and end apart: 2, of which 1 were waited for; matrix products, arithmetic and copies ran while one was open for 0% of the time, Pallas kernels for 0%

profile of v1, /device:TPU:4, one launch (start us, length us, event | category | flops | bytes accessed | tf_op | source)
XLA Modules:
  0.0 601.0 jit_solution(14249427027400156527)
XLA Ops:
  8.8 8.6 %all-to-all-start = ((f32[16,67,128]{2,1,0:T(8,128)}), f32[16,67,128]{2,1,0:T(8,128)S(1)}, u32[]{:S(2)}, u32[]{:S(2)}) async-start(f32[16,67,128]{2,1,0:T(8,128)} %stack.18), calls=%async_computation | async-start | bytes 1179648 | tf_op jit(solution)/shard_map/all_to_all | solution.py:26
  17.5 26.6 %all_gather.6 = f32[67,2048]{1,0:T(8,128)S(1)} all-gather(f32[67,128]{1,0:T(8,128)S(1)} %pad_maximum_fusion), channel_id=1, replica_groups=mesh['row'=16,'col'=16] {'row'}, dimensions={1}, use_global_device_ids=true | all-gather | bytes 583168 | tf_op jit(solution)/shard_map/all_gather | solution.py:28
  45.0 29.3 %while.57 = (s32[]{:T(128)}, f32[8,1,256]{2,1,0:T(1,128)S(1)}, s32[8]{0:T(128)S(1)}, s32[2048]{0:T(1024)S(1)}, f32[2048]{0:T(1024)S(1)}, /*index=5*/f32[2048]{0:...) while((s32[]{:T(128)}, f32[8,1,256]{2,1,0:T(1,128)S(1)}, ...), condition=%wide.region_4.5_spmd.clone, body=%wide.region_2.4_spmd.clone.sunk | while | flops 406353664 | bytes 623819 | solution.py:75
  74.3 45.2 %pmin.7 = f32[2048]{0:T(1024)S(1)} all-reduce(f32[2048]{0:T(1024)S(1)} %bitcast.148), channel_id=1, replica_groups=mesh['row'=16,'col'=16] {'col'}, use_global_device_ids=true, to_apply=%region_5.6 | all-reduce | flops 2048 | bytes 16384 | tf_op jit(solution)/shard_map/pmin | solution.py:84
  119.6 34.9 %while.58 = (s32[]{:T(128)}, f32[8,3,256]{2,1,0:T(4,128)S(1)}, s32[8]{0:T(128)S(1)}, s32[2048]{0:T(1024)S(1)}, f32[2048]{0:T(1024)S(1)}, /*index=5*/f32[2048]{0:...) while((s32[]{:T(128)}, f32[8,3,256]{2,1,0:T(4,128)S(1)}, ...), condition=%wide.region_10.11_spmd.clone, body=%wide.region_6.10_spmd.clone.sunk | while | flops 409500672 | bytes 637155 | solution.py:75
  129.8 2.9 fusion.132
  138.5 2.9 fusion.132
  142.9 2.9 fusion.132
  154.6 74.6 %all-reduce = (f32[2048]{0:T(1024)S(1)}, f32[2048]{0:T(1024)S(1)}, f32[2048]{0:T(1024)S(1)}) all-reduce(f32[2048]{0:T(1024)S(1)} %bitcast.146, f32[2048]{0:T(1024)S(1)} %bitcast.147, f32[2048]{0:T(1024)S(1)} %bitcast.145), channel_id=1, replica_groups=mesh['row'=16,'col'=16] {'col'}, use_global_device_ids=true, to_apply=%region_12.13 | all-reduce | flops 6144 | bytes 49152 | tf_op jit(solution)/shard_map/psum | solution.py:100
  229.3 32.6 %while.59 = (s32[]{:T(128)}, f32[8,1,256]{2,1,0:T(1,128)S(1)}, s32[8]{0:T(128)S(1)}, s32[2048]{0:T(1024)S(1)}, f32[2048]{0:T(1024)S(1)}, /*index=5*/f32[2048]{0:...) while((s32[]{:T(128)}, f32[8,1,256]{2,1,0:T(1,128)S(1)}, ...), condition=%wide.region_16.17_spmd.clone, body=%wide.region_14.16_spmd.clone.sunk | while | flops 407402496 | bytes 629987 | solution.py:75
  261.9 38.8 %psum.38 = f32[2048]{0:T(1024)S(1)} all-reduce(f32[2048]{0:T(1024)S(1)} %bitcast.149), channel_id=1, replica_groups=mesh['row'=16,'col'=16] {'col'}, use_global_device_ids=true, to_apply=%region_17.18 | all-reduce | flops 2048 | bytes 16384 | tf_op jit(solution)/shard_map/psum | solution.py:113
  300.8 28.0 %all_gather.7 = f32[3,2048]{1,0:T(4,128)S(1)} all-gather(f32[3,128]{1,0:T(4,128)S(1)} %pad_maximum_fusion.1), channel_id=1, replica_groups=mesh['row'=16,'col'=16] {'row'}, dimensions={1}, use_global_device_ids=true | all-gather | bytes 26112 | tf_op jit(solution)/shard_map/all_gather | solution.py:121
  328.9 34.7 %while.60 = (s32[]{:T(128)}, f32[]{:T(128)}, s32[8]{0:T(128)S(1)}, s32[2048]{0:T(1024)S(1)}, f32[2,2048]{1,0:T(2,128)S(1)}, /*index=5*/f32[2,2048]{1,0:T(2,128)S...) while((s32[]{:T(128)}, f32[]{:T(128)}, s32[8]{0:T(128)S(1)}, ...), condition=%wide.region_20.21_spmd.clone, body=%wide.region_18.20_spmd.clone.sunk | while | flops 5273607 | bytes 74971 | solution.py:132
  363.6 77.2 %psum.39 = f32[]{:T(128)} all-reduce(f32[]{:T(128)} %get-tuple-element.407), channel_id=1, replica_groups=mesh['row'=16,'col'=16] {'row','col'}, use_global_device_ids=true, to_apply=%region_21.22 | all-reduce | flops 1 | bytes 8 | tf_op jit(solution)/shard_map/psum | solution.py:135
  440.9 65.5 %while.61 = (s32[]{:T(128)}, f32[8,2,256]{2,1,0:T(2,128)S(1)}, s32[8]{0:T(128)S(1)}, f32[2,2048]{1,0:T(2,128)S(1)}, s32[2048]{0:T(1024)S(1)}, /*index=5*/f32[204...) while((s32[]{:T(128)}, f32[8,2,256]{2,1,0:T(2,128)S(1)}, ...), condition=%wide.region_24.25_spmd.clone, body=%wide.region_22.24_spmd.clone.sunk | while | flops 429423616 | bytes 4926787 | solution.py:75
  442.7 4.6 fusion.145
  450.9 4.6 fusion.145
  459.1 4.6 fusion.145
  467.3 4.6 fusion.145
  475.5 4.6 fusion.145
  483.7 4.6 fusion.145
  491.9 4.6 fusion.145
  500.1 4.6 fusion.145
  508.4 84.2 %reduce-scatter.4.cloned.1.call-done = f32[128,2]{1,0:T(8,128)} async-done(((f32[2048,2]{1,0:T(8,128)}), f32[128,2]{1,0:T(8,128)}) %reduce-scatter.4.cloned.1.call-update) | async-done | bytes 1040
  (335 shorter events, 126.8 us)
Async XLA Ops:
  8.8 35.4 %all-to-all-start = ((f32[16,67,128]{2,1,0:T(8,128)}), f32[16,67,128]{2,1,0:T(8,128)S(1)}, u32[]{:S(2)}, u32[]{:S(2)}) async-start(f32[16,67,128]{2,1,0:T(8,128)} %stack.18), calls=%async_computation | async-start | bytes 1179648 | tf_op jit(solution)/shard_map/all_to_all | solution.py:26
  17.5 575.2 %reduce-scatter.4.cloned.1.call-start = ((), (), s32[]{:S(2)}) async-start(), calls=%async_computation.2 | async-start | bytes 1114112
  44.2 0.8 copy-start
  229.3 99.6 %slice-start = ((f32[67,2048]{1,0:T(8,128)}), f32[2,2048]{1,0:T(2,128)S(1)}, s32[]{:S(2)}) async-start(f32[67,2048]{1,0:T(8,128)} %copy-done), calls=%async_computation.3 | async-start | bytes 32768 | tf_op jit(solution)/shard_map/slice | solution.py:35
Sparse Core Ops, SparseCore 0:
  507.9 84.6 reduce-scatter.3
